TPU v7x, 256 devices: a whole 4x4x8 slice. The times are simulated.
256 devices in a mesh: shot: 16 (over y_lo, z), gx: 16 (over y_hi, x, core).
Axes of the slice: x: 4, y: 4 (y_hi: 2, y_lo: 2; y = y_hi * 2 + y_lo), z: 8, core: 2. Of those that a mesh axis runs over, the one named last changes fastest.
Arguments:
- source_prev: float32 [16, 256, 64, 128], P('shot', 'gx'), may hold values from -6 to 6
- source_now: float32 [16, 256, 64, 128], P('shot', 'gx'), may hold values from -6 to 6
- receiver_prev: float32 [16, 256, 64, 128], P('shot', 'gx'), may hold values from -6 to 6
- receiver_now: float32 [16, 256, 64, 128], P('shot', 'gx'), may hold values from -6 to 6
- courant: float32 [256, 64, 128], P('gx'), may hold values from 0.05 to 0.3
- source_cells: int32 [16, 8], P('shot'), may hold values from 0 to 2097151
- wavelet: float32 [16, 2, 8], P('shot'), may hold values from -128 to 128
- receiver_cells: int32 [16, 512], P('shot'), may hold values from 0 to 2097151
- receiver_data: float32 [16, 2, 512], P('shot'), may hold values from -128 to 128
- offsets: int32 [9], replicated, may hold values from -8 to 8, as said below
- conv_weight: float32 [64, 9, 3, 3, 3], replicated, may hold values from -1.25 to 1.25
- conv_bias: float32 [64], replicated, may hold values from -3 to 3
Outputs:
- summary: float32 [64, 64, 512], P(None, 'gx', 'shot')
Inputs may be any that keep to these rules, and one draw needn't show every extreme that they name: The offsets are distinct and include -8 and 8.
All inputs are finite; a program needn't handle non-finite values.
Results may differ from a plain program's by a relative error of at most 0.0003.
Values sent between devices are 32-bit elements; how exact they have to be, the bound alone decides.
No kernel may reach another device: no remote copies, remote signals or barrier semaphores. Data moves between devices by JAX's collectives and lax.ppermute only.
A program may use at most 64 MiB of HBM per device.

v0:
```python
import jax
import jax.numpy as jnp
from jax import lax
from jax.sharding import PartitionSpec as P

HMAX = 8


def padded_2(block, sides, width):
    for axis, dim in sides:
        count = lax.axis_size(axis)
        forward = [(i, i + 1) for i in range(count - 1)]
        backward = [(target, source) for source, target in forward]
        low = lax.ppermute(
            lax.slice_in_dim(block, block.shape[dim] - width, None, axis=dim), axis, forward
        )
        high = lax.ppermute(lax.slice_in_dim(block, 0, width, axis=dim), axis, backward)
        block = jnp.concatenate([low, block, high], axis=dim)
    return block


def inject(cells_here, first_x, cell_index, amplitudes, size_y, size_z):
    plane_size = size_y * size_z
    column = cell_index // plane_size
    within = cell_index % plane_size
    local_x = column - first_x
    inside = (local_x >= 0) & (local_x < cells_here)
    target = jnp.where(inside, local_x * plane_size + within, cells_here * plane_size)
    flat_cells = jnp.zeros((cells_here * plane_size + 1,), jnp.float32).at[target].add(amplitudes)
    return flat_cells[:-1].reshape(cells_here, size_y, size_z)


def laplace_step(previous, extended, courant, sources):
    center = extended[:, 1:-1]
    padded = jnp.pad(center, ((0, 0), (0, 0), (1, 1), (1, 1)))
    laplace = extended[:, 2:] + extended[:, :-2]
    laplace = laplace + padded[:, :, 2:, 1:-1] + padded[:, :, :-2, 1:-1]
    laplace = laplace + padded[:, :, 1:-1, 2:] + padded[:, :, 1:-1, :-2] - 6.0 * center
    return 2.0 * center - previous + courant * laplace + sources


def coarsen(image_block):
    size_x, size_y, size_z = image_block.shape
    return image_block.reshape(size_x // 4, 4, size_y // 4, 4, size_z // 4, 4).mean(axis=(1, 3, 5))


def offset_image(wide, offsets, margin, cells_x):

    def per_offset(offset_value):
        forward_part = lax.dynamic_slice_in_dim(wide, margin + offset_value, cells_x, 1)
        backward_part = lax.dynamic_slice_in_dim(wide, margin - offset_value, cells_x, 1)
        image_block = forward_part[0] * backward_part[1] + forward_part[2] * backward_part[3]
        return coarsen(image_block)

    return lax.map(per_offset, offsets)


def conv_apply(padded, conv_weight, conv_bias):
    channels, span_x, span_y, span_z = padded.shape
    size_x, size_y, size_z = (span_x - 2, span_y - 2, span_z - 2)
    patches = jnp.stack(
        [
            padded[:, step_x : step_x + size_x, step_y : step_y + size_y, step_z : step_z + size_z]
            for step_x in range(3)
            for step_y in range(3)
            for step_z in range(3)
        ],
        axis=1,
    )
    patches = patches.reshape(channels * 27, size_x * size_y * size_z)
    matrix = conv_weight.reshape(conv_weight.shape[0], channels * 27)
    result = jnp.dot(
        matrix, patches, precision=lax.Precision.HIGHEST, preferred_element_type=jnp.float32
    )
    result = result + conv_bias[:, None]
    return result.reshape(conv_weight.shape[0], size_x, size_y * size_z)


def local(
    source_prev,
    source_now,
    receiver_prev,
    receiver_now,
    courant,
    source_cells,
    wavelet,
    receiver_cells,
    receiver_data,
    offsets,
    conv_weight,
    conv_bias,
):
    cells_x, size_y, size_z = courant.shape
    slab_index = lax.axis_index("gx")
    previous = jnp.stack([source_prev[0], receiver_prev[0]])
    current = jnp.stack([source_now[0], receiver_now[0]])
    levels = []
    for step_index in range(2):
        extended = padded_2(current, (("gx", 1),), 1)
        first_x = slab_index * cells_x
        advanced = laplace_step(
            previous,
            extended,
            courant,
            jnp.stack(
                [
                    inject(
                        cells_x, first_x, source_cells[0], wavelet[0, step_index], size_y, size_z
                    ),
                    inject(
                        cells_x,
                        first_x,
                        receiver_cells[0],
                        receiver_data[0, step_index],
                        size_y,
                        size_z,
                    ),
                ]
            ),
        )
        previous, current = (current, advanced)
        levels.append(advanced)
    fields = jnp.concatenate(levels, axis=0)
    wide = padded_2(fields, (("gx", 1),), HMAX)
    coarse = offset_image(wide, offsets, HMAX, cells_x)
    summed = lax.psum(coarse, "shot")
    rimmed = padded_2(summed, (("gx", 1),), 1)
    row_count = summed.shape[2] // lax.axis_size("shot")
    padded = jnp.pad(rimmed, ((0, 0), (0, 0), (1, 1), (1, 1)))
    window = lax.dynamic_slice_in_dim(padded, lax.axis_index("shot") * row_count, row_count + 2, 2)
    return conv_apply(window, conv_weight, conv_bias)


def solution(mesh):
    in_specs = (
        P("shot", "gx", None, None),
        P("shot", "gx", None, None),
        P("shot", "gx", None, None),
        P("shot", "gx", None, None),
        P("gx", None, None),
        P("shot", None),
        P("shot", None, None),
        P("shot", None),
        P("shot", None, None),
        P(),
        P(),
        P(),
    )
    out_specs = P(None, "gx", "shot")
    return jax.shard_map(local, mesh=mesh, in_specs=in_specs, out_specs=out_specs, check_vma=False)
```

profile of v0, /device:TPU:7, one launch (start us, length us, event | category | flops | bytes accessed | tf_op | source)
XLA Modules:
  0.0 510.2 jit_solution(17402110244412481747)
XLA Ops:
  6.5 1.1 constant_dynamic-update-slice_fusion.1
  7.7 1.1 constant_dynamic-update-slice_fusion
  8.8 2.6 collective-permute-start
  11.4 6.6 %collective-permute-start.1 = (f32[2,1,64,128]{3,2,1,0:T(8,128)S(1)}, f32[2,1,64,128]{3,2,1,0:T(8,128)S(1)}, u32[]{:S(2)}, u32[]{:S(2)}) collective-permute-start(f32[2,1,64,128]{3,2,1,0:T(8,128)S(1)} %get-tuple-element.86), channel_id=1, source_target_pairs={{0,1},{1,2},{2,3},{3,4},{4,5},{5,6},{6,7},{7,8},{8,9},{9,10},{10,1... | collective-permute-start | bytes 196616 | tf_op jit(solution)/shard_map/ppermute | solution.py:14
  18.0 0.8 fusion.52
  18.7 0.8 slice_bitcast_fusion
  19.5 0.7 compare_select_fusion
  20.2 0.7 fusion.46
  20.9 4.0 scatter_custom_fusion.1
  25.0 0.7 scatter_custom_fusion
  25.8 1.9 fusion.10
  27.7 1.9 collective-permute-start.2
  29.7 7.3 %collective-permute-start.3 = (f32[2,1,64,128]{3,2,1,0:T(8,128)S(1)}, f32[2,1,64,128]{3,2,1,0:T(8,128)S(1)}, u32[]{:S(2)}, u32[]{:S(2)}) collective-permute-start(f32[2,1,64,128]{3,2,1,0:T(8,128)S(1)} %get-tuple-element.84), channel_id=1, source_target_pairs={{0,1},{1,2},{2,3},{3,4},{4,5},{5,6},{6,7},{7,8},{8,9},{9,10},{10,1... | collective-permute-start | bytes 196616 | tf_op jit(solution)/shard_map/ppermute | solution.py:14
  36.9 4.0 scatter_custom_fusion.3
  41.0 0.8 slice.259
  41.8 0.7 scatter_custom_fusion.2
  42.6 1.9 fusion.18
  44.5 1.2 fusion.2
  45.7 3.5 collective-permute-start.4
  49.2 1.9 collective-permute-start.5
  51.2 10.1 %collective-permute-done.4 = f32[4,8,64,128]{3,2,1,0:T(8,128)} collective-permute-done((f32[4,8,64,128]{3,2,1,0:T(8,128)}, f32[4,8,64,128]{3,2,1,0:T(8,128)}, u32[]{:S(2)}, u32[]{:S(2)}) %collective-permute-start.4) | collective-permute-done | bytes 1048608 | tf_op jit(solution)/shard_map/ppermute | solution.py:14
  61.3 7.8 %collective-permute-done.5 = f32[4,8,64,128]{3,2,1,0:T(8,128)} collective-permute-done((f32[4,8,64,128]{3,2,1,0:T(8,128)S(1)}, f32[4,8,64,128]{3,2,1,0:T(8,128)}, u32[]{:S(2)}, u32[]{:S(2)}) %collective-permute-start.5) | collective-permute-done | bytes 1048608 | tf_op jit(solution)/shard_map/ppermute | solution.py:17
  69.1 4.0 pad_maximum_fusion
  73.1 277.4 %while.13 = (s32[]{:T(128)}, f32[9,4,16,32]{3,2,1,0:T(8,128)}, s32[9]{0:T(128)S(1)}, f32[4,32,64,128]{3,2,1,0:T(8,128)}, s32[]{:T(128)}, /*index=5*/s32[]{:T(128...) while((s32[]{:T(128)}, f32[9,4,16,32]{3,2,1,0:T(8,128)}, s32[9]{0:T(128)S(1)}, ...), condition=%wide.region_6.7_spmd, body=%wide.region_4.6_spmd.sunk | while | flops 524301 | bytes 4244249 | solution.py:55
  75.9 1.7 fusion.56
  77.6 18.6 %add.415 = f32[4,4,16,4,32,4]{5,4,3,2,1,0:T(8,128)} reshape(f32[1,16,64,128]{3,2,1,0:T(8,128)S(1)} %fusion.56) | data formatting | bytes 1048576 | tf_op jit(solution)/shard_map/while/body/eval_jaxpr/add | solution.py:52
  96.2 7.1 %reduce_sum.14 = f32[4,16,32]{2,1,0:T(8,128)S(1)} reduce(f32[4,4,16,4,32,4]{5,4,3,2,1,0:T(8,128)} %add.415, f32[]{:T(128)} %constant.122.clone.1..sunk), dimensions={1,3,5}, to_apply=%region_5.5 | reduce | flops 129024 | bytes 532484 | tf_op jit(solution)/shard_map/while/body/eval_jaxpr/reduce_sum | solution.py:44
  106.7 1.7 fusion.56
  108.4 18.6 %add.415 = f32[4,4,16,4,32,4]{5,4,3,2,1,0:T(8,128)} reshape(f32[1,16,64,128]{3,2,1,0:T(8,128)S(1)} %fusion.56) | data formatting | bytes 1048576 | tf_op jit(solution)/shard_map/while/body/eval_jaxpr/add | solution.py:52
  127.0 7.1 %reduce_sum.14 = f32[4,16,32]{2,1,0:T(8,128)S(1)} reduce(f32[4,4,16,4,32,4]{5,4,3,2,1,0:T(8,128)} %add.415, f32[]{:T(128)} %constant.122.clone.1..sunk), dimensions={1,3,5}, to_apply=%region_5.5 | reduce | flops 129024 | bytes 532484 | tf_op jit(solution)/shard_map/while/body/eval_jaxpr/reduce_sum | solution.py:44
  137.5 1.7 fusion.56
  139.2 18.6 %add.415 = f32[4,4,16,4,32,4]{5,4,3,2,1,0:T(8,128)} reshape(f32[1,16,64,128]{3,2,1,0:T(8,128)S(1)} %fusion.56) | data formatting | bytes 1048576 | tf_op jit(solution)/shard_map/while/body/eval_jaxpr/add | solution.py:52
  157.9 7.1 %reduce_sum.14 = f32[4,16,32]{2,1,0:T(8,128)S(1)} reduce(f32[4,4,16,4,32,4]{5,4,3,2,1,0:T(8,128)} %add.415, f32[]{:T(128)} %constant.122.clone.1..sunk), dimensions={1,3,5}, to_apply=%region_5.5 | reduce | flops 129024 | bytes 532484 | tf_op jit(solution)/shard_map/while/body/eval_jaxpr/reduce_sum | solution.py:44
  164.9 0.6 bitcast_dynamic-update-slice_fusion.2
  168.3 1.7 fusion.56
  170.0 18.6 %add.415 = f32[4,4,16,4,32,4]{5,4,3,2,1,0:T(8,128)} reshape(f32[1,16,64,128]{3,2,1,0:T(8,128)S(1)} %fusion.56) | data formatting | bytes 1048576 | tf_op jit(solution)/shard_map/while/body/eval_jaxpr/add | solution.py:52
  188.7 7.1 %reduce_sum.14 = f32[4,16,32]{2,1,0:T(8,128)S(1)} reduce(f32[4,4,16,4,32,4]{5,4,3,2,1,0:T(8,128)} %add.415, f32[]{:T(128)} %constant.122.clone.1..sunk), dimensions={1,3,5}, to_apply=%region_5.5 | reduce | flops 129024 | bytes 532484 | tf_op jit(solution)/shard_map/while/body/eval_jaxpr/reduce_sum | solution.py:44
  195.7 0.6 bitcast_dynamic-update-slice_fusion.2
  199.2 1.7 fusion.56
  200.8 18.6 %add.415 = f32[4,4,16,4,32,4]{5,4,3,2,1,0:T(8,128)} reshape(f32[1,16,64,128]{3,2,1,0:T(8,128)S(1)} %fusion.56) | data formatting | bytes 1048576 | tf_op jit(solution)/shard_map/while/body/eval_jaxpr/add | solution.py:52
  219.5 7.1 %reduce_sum.14 = f32[4,16,32]{2,1,0:T(8,128)S(1)} reduce(f32[4,4,16,4,32,4]{5,4,3,2,1,0:T(8,128)} %add.415, f32[]{:T(128)} %constant.122.clone.1..sunk), dimensions={1,3,5}, to_apply=%region_5.5 | reduce | flops 129024 | bytes 532484 | tf_op jit(solution)/shard_map/while/body/eval_jaxpr/reduce_sum | solution.py:44
  226.6 0.6 bitcast_dynamic-update-slice_fusion.2
  230.0 1.7 fusion.56
  231.7 18.6 %add.415 = f32[4,4,16,4,32,4]{5,4,3,2,1,0:T(8,128)} reshape(f32[1,16,64,128]{3,2,1,0:T(8,128)S(1)} %fusion.56) | data formatting | bytes 1048576 | tf_op jit(solution)/shard_map/while/body/eval_jaxpr/add | solution.py:52
  250.3 7.1 %reduce_sum.14 = f32[4,16,32]{2,1,0:T(8,128)S(1)} reduce(f32[4,4,16,4,32,4]{5,4,3,2,1,0:T(8,128)} %add.415, f32[]{:T(128)} %constant.122.clone.1..sunk), dimensions={1,3,5}, to_apply=%region_5.5 | reduce | flops 129024 | bytes 532484 | tf_op jit(solution)/shard_map/while/body/eval_jaxpr/reduce_sum | solution.py:44
  257.4 0.6 bitcast_dynamic-update-slice_fusion.2
  260.8 1.7 fusion.56
  262.5 18.6 %add.415 = f32[4,4,16,4,32,4]{5,4,3,2,1,0:T(8,128)} reshape(f32[1,16,64,128]{3,2,1,0:T(8,128)S(1)} %fusion.56) | data formatting | bytes 1048576 | tf_op jit(solution)/shard_map/while/body/eval_jaxpr/add | solution.py:52
  281.1 7.1 %reduce_sum.14 = f32[4,16,32]{2,1,0:T(8,128)S(1)} reduce(f32[4,4,16,4,32,4]{5,4,3,2,1,0:T(8,128)} %add.415, f32[]{:T(128)} %constant.122.clone.1..sunk), dimensions={1,3,5}, to_apply=%region_5.5 | reduce | flops 129024 | bytes 532484 | tf_op jit(solution)/shard_map/while/body/eval_jaxpr/reduce_sum | solution.py:44
  291.6 1.7 fusion.56
  293.3 18.6 %add.415 = f32[4,4,16,4,32,4]{5,4,3,2,1,0:T(8,128)} reshape(f32[1,16,64,128]{3,2,1,0:T(8,128)S(1)} %fusion.56) | data formatting | bytes 1048576 | tf_op jit(solution)/shard_map/while/body/eval_jaxpr/add | solution.py:52
  312.0 7.1 %reduce_sum.14 = f32[4,16,32]{2,1,0:T(8,128)S(1)} reduce(f32[4,4,16,4,32,4]{5,4,3,2,1,0:T(8,128)} %add.415, f32[]{:T(128)} %constant.122.clone.1..sunk), dimensions={1,3,5}, to_apply=%region_5.5 | reduce | flops 129024 | bytes 532484 | tf_op jit(solution)/shard_map/while/body/eval_jaxpr/reduce_sum | solution.py:44
  319.0 0.6 bitcast_dynamic-update-slice_fusion.2
  322.4 1.7 fusion.56
  324.1 18.6 %add.415 = f32[4,4,16,4,32,4]{5,4,3,2,1,0:T(8,128)} reshape(f32[1,16,64,128]{3,2,1,0:T(8,128)S(1)} %fusion.56) | data formatting | bytes 1048576 | tf_op jit(solution)/shard_map/while/body/eval_jaxpr/add | solution.py:52
  342.8 7.1 %reduce_sum.14 = f32[4,16,32]{2,1,0:T(8,128)S(1)} reduce(f32[4,4,16,4,32,4]{5,4,3,2,1,0:T(8,128)} %add.415, f32[]{:T(128)} %constant.122.clone.1..sunk), dimensions={1,3,5}, to_apply=%region_5.5 | reduce | flops 129024 | bytes 532484 | tf_op jit(solution)/shard_map/while/body/eval_jaxpr/reduce_sum | solution.py:44
  349.8 0.6 bitcast_dynamic-update-slice_fusion.2
  350.5 123.0 %all-reduce.5.cloned.1.call-done = f32[9,4,16,32]{3,2,1,0:T(8,128)} async-done(((f32[9,4,16,32]{3,2,1,0:T(8,128)}), f32[9,4,16,32]{3,2,1,0:T(8,128)}) %all-reduce.5.cloned.1.call-update) | async-done | bytes 73744 | tf_op jit(solution)/shard_map/psum | solution.py:126
  473.5 0.9 fusion.49
  474.4 15.8 %collective-permute-start.6 = (f32[9,1,16,32]{3,2,1,0:T(8,128)S(1)}, f32[9,1,16,32]{3,2,1,0:T(8,128)S(1)}, u32[]{:S(2)}, u32[]{:S(2)}) collective-permute-start(f32[9,1,16,32]{3,2,1,0:T(8,128)S(1)} %get-tuple-element.88), channel_id=1, source_target_pairs={{0,1},{1,2},{2,3},{3,4},{4,5},{5,6},{6,7},{7,8},{8,9},{9,10},{10,1... | collective-permute-start | bytes 55304 | tf_op jit(solution)/shard_map/ppermute | solution.py:14
  490.2 1.9 collective-permute-start.7
  492.3 7.2 %collective-permute-done.7 = f32[9,1,16,32]{3,2,1,0:T(8,128)S(1)} collective-permute-done((f32[9,1,16,32]{3,2,1,0:T(8,128)S(1)}, f32[9,1,16,32]{3,2,1,0:T(8,128)S(1)}, u32[]{:S(2)}, u32[]{:S(2)}) %collective-permute-start.7) | collective-permute-done | bytes 18464 | tf_op jit(solution)/shard_map/ppermute | solution.py:17
  499.5 1.2 fusion.36
  502.7 0.7 copy.67
  (67 shorter events, 9.1 us)
Async XLA Ops:
  6.5 19.2 %copy-start = (f32[16,64,128]{2,1,0:T(8,128)S(1)}, f32[16,64,128]{2,1,0:T(8,128)}, u32[]{:S(2)}) copy-start(f32[16,64,128]{2,1,0:T(8,128)} %param.18) | copy-start | bytes 1572868
  6.5 466.9 %all-reduce.5.cloned.1.call-start = ((), (), s32[]{:S(2)}) async-start(), calls=%async_computation | async-start | bytes 589824 | tf_op jit(solution)/shard_map/psum | solution.py:126
  8.8 17.0 %collective-permute-start = (f32[2,1,64,128]{3,2,1,0:T(8,128)S(1)}, f32[2,1,64,128]{3,2,1,0:T(8,128)S(1)}, u32[]{:S(2)}, u32[]{:S(2)}) collective-permute-start(f32[2,1,64,128]{3,2,1,0:T(8,128)S(1)} %get-tuple-element.85), channel_id=1, source_target_pairs={{1,0},{2,1},{3,2},{4,3},{5,4},{6,5},{7,6},{8,7},{9,8},{10,9},{11,1... | collective-permute-start | bytes 196616 | tf_op jit(solution)/shard_map/ppermute | solution.py:17
  11.4 14.4 %collective-permute-start.1 = (f32[2,1,64,128]{3,2,1,0:T(8,128)S(1)}, f32[2,1,64,128]{3,2,1,0:T(8,128)S(1)}, u32[]{:S(2)}, u32[]{:S(2)}) collective-permute-start(f32[2,1,64,128]{3,2,1,0:T(8,128)S(1)} %get-tuple-element.86), channel_id=1, source_target_pairs={{0,1},{1,2},{2,3},{3,4},{4,5},{5,6},{6,7},{7,8},{8,9},{9,10},{10,1... | collective-permute-start | bytes 196616 | tf_op jit(solution)/shard_map/ppermute | solution.py:14
  27.7 14.8 %collective-permute-start.2 = (f32[2,1,64,128]{3,2,1,0:T(8,128)S(1)}, f32[2,1,64,128]{3,2,1,0:T(8,128)S(1)}, u32[]{:S(2)}, u32[]{:S(2)}) collective-permute-start(f32[2,1,64,128]{3,2,1,0:T(8,128)S(1)} %get-tuple-element.83), channel_id=1, source_target_pairs={{1,0},{2,1},{3,2},{4,3},{5,4},{6,5},{7,6},{8,7},{9,8},{10,9},{11,1... | collective-permute-start | bytes 196616 | tf_op jit(solution)/shard_map/ppermute | solution.py:17
  29.7 12.9 %collective-permute-start.3 = (f32[2,1,64,128]{3,2,1,0:T(8,128)S(1)}, f32[2,1,64,128]{3,2,1,0:T(8,128)S(1)}, u32[]{:S(2)}, u32[]{:S(2)}) collective-permute-start(f32[2,1,64,128]{3,2,1,0:T(8,128)S(1)} %get-tuple-element.84), channel_id=1, source_target_pairs={{0,1},{1,2},{2,3},{3,4},{4,5},{5,6},{6,7},{7,8},{8,9},{9,10},{10,1... | collective-permute-start | bytes 196616 | tf_op jit(solution)/shard_map/ppermute | solution.py:14
  45.7 15.6 %collective-permute-start.4 = (f32[4,8,64,128]{3,2,1,0:T(8,128)}, f32[4,8,64,128]{3,2,1,0:T(8,128)}, u32[]{:S(2)}, u32[]{:S(2)}) collective-permute-start(f32[4,8,64,128]{3,2,1,0:T(8,128)} %get-tuple-element.81), channel_id=1, source_target_pairs={{0,1},{1,2},{2,3},{3,4},{4,5},{5,6},{6,7},{7,8},{8,9},{9,10},{10,1... | collective-permute-start | bytes 3145736 | tf_op jit(solution)/shard_map/ppermute | solution.py:14
  49.2 19.8 %collective-permute-start.5 = (f32[4,8,64,128]{3,2,1,0:T(8,128)S(1)}, f32[4,8,64,128]{3,2,1,0:T(8,128)}, u32[]{:S(2)}, u32[]{:S(2)}) collective-permute-start(f32[4,8,64,128]{3,2,1,0:T(8,128)S(1)} %get-tuple-element.82), channel_id=1, source_target_pairs={{1,0},{2,1},{3,2},{4,3},{5,4},{6,5},{7,6},{8,7},{9,8},{10,9},{11,1... | collective-permute-start | bytes 3145736 | tf_op jit(solution)/shard_map/ppermute | solution.py:17
  51.2 21.9 %copy-start.3 = (s32[9]{0:T(128)S(1)}, s32[9]{0:T(128)}, u32[]{:S(2)}) copy-start(s32[9]{0:T(128)} %param.23) | copy-start | bytes 112
  73.1 419.2 %copy-start.1 = (f32[64,9,3,3,3]{0,4,3,2,1:T(4,128)S(1)}, f32[64,9,3,3,3]{0,4,3,2,1:T(4,128)}, u32[]{:S(2)}) copy-start(f32[64,9,3,3,3]{0,4,3,2,1:T(4,128)} %param.24) | copy-start | bytes 186628
  350.4 151.8 %copy-start.2 = (f32[64]{0:T(128)S(1)}, f32[64]{0:T(128)}, u32[]{:S(2)}) copy-start(f32[64]{0:T(128)} %param.25) | copy-start | bytes 772
  474.4 17.9 %collective-permute-start.6 = (f32[9,1,16,32]{3,2,1,0:T(8,128)S(1)}, f32[9,1,16,32]{3,2,1,0:T(8,128)S(1)}, u32[]{:S(2)}, u32[]{:S(2)}) collective-permute-start(f32[9,1,16,32]{3,2,1,0:T(8,128)S(1)} %get-tuple-element.88), channel_id=1, source_target_pairs={{0,1},{1,2},{2,3},{3,4},{4,5},{5,6},{6,7},{7,8},{8,9},{9,10},{10,1... | collective-permute-start | bytes 55304 | tf_op jit(solution)/shard_map/ppermute | solution.py:14
  490.2 9.3 %collective-permute-start.7 = (f32[9,1,16,32]{3,2,1,0:T(8,128)S(1)}, f32[9,1,16,32]{3,2,1,0:T(8,128)S(1)}, u32[]{:S(2)}, u32[]{:S(2)}) collective-permute-start(f32[9,1,16,32]{3,2,1,0:T(8,128)S(1)} %get-tuple-element.87), channel_id=1, source_target_pairs={{1,0},{2,1},{3,2},{4,3},{5,4},{6,5},{7,6},{8,7},{9,8},{10,9},{11,1... | collective-permute-start | bytes 55304 | tf_op jit(solution)/shard_map/ppermute | solution.py:17
Sparse Core Ops, SparseCore 0:
  350.6 122.8 all-reduce.4
where the time goes:
time: 512 us; the launch traced here: 510 us
  local copies, waits for them, and re-layouts  181 us (35%)
  waiting for transfers between devices  148 us (29%)
  other arithmetic  105 us (21%)
  starting transfers between devices  41.5 us (8%)
  loops' own time  20.3 us (4%)
  between operations  13.8 us (3%)
    add x9, local copies, waits for them, and re-layouts, per_offset(): forward_part[0] * backward_part[1] + forward_part[2] * backward_part[3]  168 us
    psum x1, waiting for transfers between devices, local(): summed = lax.psum(coarse, 'shot')  123 us
    reduce_sum x9, other arithmetic, coarsen(): image_block.reshape(size_x // 4, 4, size_y // 4, 4, size_z // 4, 4)  63.6 us
    ppermute x4, starting transfers between devices, padded_2(): lax.ppermute(lax.slice_in_dim(block, block.shape[dim] - width, None, axis...  33.2 us
    another operation x1, loops' own time, offset_image(): return lax.map(per_offset, offsets)  20.3 us
    add x9, other arithmetic, per_offset(): forward_part[0] * backward_part[1] + forward_part[2] * backward_part[3]  15.1 us
    ppermute x4, waiting for transfers between devices, padded_2(): lax.ppermute(lax.slice_in_dim(block, 0, width, axis=dim), axis, backward)  15 us
  transfers between devices with their start and end apart: 9, of which 4 were waited for; matrix products, arithmetic and copies ran while one was open for 3% of the time, Pallas kernels for 0%

commit v1 on v0

--- a/solution.py
+++ b/solution.py
@@ -1,9 +1,19 @@
+import functools
 import jax
 import jax.numpy as jnp
 from jax import lax
 from jax.sharding import PartitionSpec as P
+from jax.lax import all_gather
 
 HMAX = 8
+
+
+def leaves_close(sheet, which_axis):
+    response = jnp.sum(all_gather(sheet, which_axis), axis=0)
+    return response
+
+
+signs_update = functools.partial(leaves_close, which_axis="shot")
 
 
 def padded_2(block, sides, width):
@@ -123,7 +133,7 @@
     fields = jnp.concatenate(levels, axis=0)
     wide = padded_2(fields, (("gx", 1),), HMAX)
     coarse = offset_image(wide, offsets, HMAX, cells_x)
-    summed = lax.psum(coarse, "shot")
+    summed = signs_update(coarse)
     rimmed = padded_2(summed, (("gx", 1),), 1)
     row_count = summed.shape[2] // lax.axis_size("shot")
     padded = jnp.pad(rimmed, ((0, 0), (0, 0), (1, 1), (1, 1)))

time: 512 us -> 456 us (0.89)
  waiting for transfers between devices: 148 us -> 93.2 us
    psum x1 -> x0, waiting for transfers between devices: 123 us -> none  [local(): summed = lax.psum(coarse, 'shot')]
    all_gather x0 -> x1, waiting for transfers between devices: none -> 68.1 us  [leaves_close(): response = jnp.sum(all_gather(sheet, which_axis), axis=0)]
where the time goes in v1:
time: 456 us; the launch traced here: 455 us
  local copies, waits for them, and re-layouts  180 us (39%)
  other arithmetic  107 us (23%)
  waiting for transfers between devices  93.2 us (20%)
  starting transfers between devices  39.9 us (9%)
  loops' own time  20.3 us (4%)
  between operations  13.8 us (3%)
    add x9, local copies, waits for them, and re-layouts, per_offset(): forward_part[0] * backward_part[1] + forward_part[2] * backward_part[3]  168 us
    all_gather x1, waiting for transfers between devices, leaves_close(): response = jnp.sum(all_gather(sheet, which_axis), axis=0)  68.1 us
    reduce_sum x9, other arithmetic, coarsen(): image_block.reshape(size_x // 4, 4, size_y // 4, 4, size_z // 4, 4)  63.6 us
    ppermute x4, starting transfers between devices, padded_2(): lax.ppermute(lax.slice_in_dim(block, block.shape[dim] - width, None, axis...  31.6 us
    another operation x1, loops' own time, offset_image(): return lax.map(per_offset, offsets)  20.3 us
    add x9, other arithmetic, per_offset(): forward_part[0] * backward_part[1] + forward_part[2] * backward_part[3]  15.1 us
    ppermute x4, waiting for transfers between devices, padded_2(): lax.ppermute(lax.slice_in_dim(block, 0, width, axis=dim), axis, backward)  15 us
    ppermute x4, waiting for transfers between devices, padded_2(): lax.ppermute(lax.slice_in_dim(block, block.shape[dim] - width, None, axis...  10.1 us
  transfers between devices with their start and end apart: 9, of which 4 were waited for; matrix products, arithmetic and copies ran while one was open for 3% of the time, Pallas kernels for 0%

profile of v1, /device:TPU:7, one launch (start us, length us, event | category | flops | bytes accessed | tf_op | source)
XLA Modules:
  0.0 454.8 jit_solution(6510357783216687768)
XLA Ops:
  6.5 1.1 constant_dynamic-update-slice_fusion.1
  7.7 1.1 constant_dynamic-update-slice_fusion
  8.8 2.6 collective-permute-start
  11.4 6.6 %collective-permute-start.1 = (f32[2,1,64,128]{3,2,1,0:T(8,128)S(1)}, f32[2,1,64,128]{3,2,1,0:T(8,128)S(1)}, u32[]{:S(2)}, u32[]{:S(2)}) collective-permute-start(f32[2,1,64,128]{3,2,1,0:T(8,128)S(1)} %get-tuple-element.86), channel_id=1, source_target_pairs={{0,1},{1,2},{2,3},{3,4},{4,5},{5,6},{6,7},{7,8},{8,9},{9,10},{10,1... | collective-permute-start | bytes 196616 | tf_op jit(solution)/shard_map/ppermute | solution.py:24
  18.0 0.8 fusion.52
  18.7 0.8 slice_bitcast_fusion
  19.5 0.7 compare_select_fusion
  20.2 0.7 fusion.46
  20.9 4.0 scatter_custom_fusion.1
  25.0 0.7 scatter_custom_fusion
  25.8 1.9 fusion.10
  27.7 1.9 collective-permute-start.2
  29.7 7.3 %collective-permute-start.3 = (f32[2,1,64,128]{3,2,1,0:T(8,128)S(1)}, f32[2,1,64,128]{3,2,1,0:T(8,128)S(1)}, u32[]{:S(2)}, u32[]{:S(2)}) collective-permute-start(f32[2,1,64,128]{3,2,1,0:T(8,128)S(1)} %get-tuple-element.84), channel_id=1, source_target_pairs={{0,1},{1,2},{2,3},{3,4},{4,5},{5,6},{6,7},{7,8},{8,9},{9,10},{10,1... | collective-permute-start | bytes 196616 | tf_op jit(solution)/shard_map/ppermute | solution.py:24
  36.9 4.0 scatter_custom_fusion.3
  41.0 0.8 slice.259
  41.8 0.7 scatter_custom_fusion.2
  42.6 1.9 fusion.18
  44.5 1.2 fusion.2
  45.7 3.5 collective-permute-start.4
  49.2 1.9 collective-permute-start.5
  51.2 10.1 %collective-permute-done.4 = f32[4,8,64,128]{3,2,1,0:T(8,128)} collective-permute-done((f32[4,8,64,128]{3,2,1,0:T(8,128)}, f32[4,8,64,128]{3,2,1,0:T(8,128)}, u32[]{:S(2)}, u32[]{:S(2)}) %collective-permute-start.4) | collective-permute-done | bytes 1048608 | tf_op jit(solution)/shard_map/ppermute | solution.py:24
  61.3 7.8 %collective-permute-done.5 = f32[4,8,64,128]{3,2,1,0:T(8,128)} collective-permute-done((f32[4,8,64,128]{3,2,1,0:T(8,128)S(1)}, f32[4,8,64,128]{3,2,1,0:T(8,128)}, u32[]{:S(2)}, u32[]{:S(2)}) %collective-permute-start.5) | collective-permute-done | bytes 1048608 | tf_op jit(solution)/shard_map/ppermute | solution.py:27
  69.1 4.0 pad_maximum_fusion
  73.1 277.4 %while.13 = (s32[]{:T(128)}, f32[9,4,16,32]{3,2,1,0:T(8,128)}, s32[9]{0:T(128)S(1)}, f32[4,32,64,128]{3,2,1,0:T(8,128)}, s32[]{:T(128)}, /*index=5*/s32[]{:T(128...) while((s32[]{:T(128)}, f32[9,4,16,32]{3,2,1,0:T(8,128)}, s32[9]{0:T(128)S(1)}, ...), condition=%wide.region_6.7_spmd, body=%wide.region_4.6_spmd.sunk | while | flops 524301 | bytes 4244249 | solution.py:65
  75.9 1.7 fusion.56
  77.6 18.6 %add.413 = f32[4,4,16,4,32,4]{5,4,3,2,1,0:T(8,128)} reshape(f32[1,16,64,128]{3,2,1,0:T(8,128)S(1)} %fusion.56) | data formatting | bytes 1048576 | tf_op jit(solution)/shard_map/while/body/eval_jaxpr/add | solution.py:62
  96.2 7.1 %reduce_sum.24 = f32[4,16,32]{2,1,0:T(8,128)S(1)} reduce(f32[4,4,16,4,32,4]{5,4,3,2,1,0:T(8,128)} %add.413, f32[]{:T(128)} %constant.123.clone.1..sunk), dimensions={1,3,5}, to_apply=%region_5.5 | reduce | flops 129024 | bytes 532484 | tf_op jit(solution)/shard_map/while/body/eval_jaxpr/reduce_sum | solution.py:54
  106.7 1.7 fusion.56
  108.4 18.6 %add.413 = f32[4,4,16,4,32,4]{5,4,3,2,1,0:T(8,128)} reshape(f32[1,16,64,128]{3,2,1,0:T(8,128)S(1)} %fusion.56) | data formatting | bytes 1048576 | tf_op jit(solution)/shard_map/while/body/eval_jaxpr/add | solution.py:62
  127.0 7.1 %reduce_sum.24 = f32[4,16,32]{2,1,0:T(8,128)S(1)} reduce(f32[4,4,16,4,32,4]{5,4,3,2,1,0:T(8,128)} %add.413, f32[]{:T(128)} %constant.123.clone.1..sunk), dimensions={1,3,5}, to_apply=%region_5.5 | reduce | flops 129024 | bytes 532484 | tf_op jit(solution)/shard_map/while/body/eval_jaxpr/reduce_sum | solution.py:54
  134.1 0.6 bitcast_dynamic-update-slice_fusion.2
  137.5 1.7 fusion.56
  139.2 18.6 %add.413 = f32[4,4,16,4,32,4]{5,4,3,2,1,0:T(8,128)} reshape(f32[1,16,64,128]{3,2,1,0:T(8,128)S(1)} %fusion.56) | data formatting | bytes 1048576 | tf_op jit(solution)/shard_map/while/body/eval_jaxpr/add | solution.py:62
  157.9 7.1 %reduce_sum.24 = f32[4,16,32]{2,1,0:T(8,128)S(1)} reduce(f32[4,4,16,4,32,4]{5,4,3,2,1,0:T(8,128)} %add.413, f32[]{:T(128)} %constant.123.clone.1..sunk), dimensions={1,3,5}, to_apply=%region_5.5 | reduce | flops 129024 | bytes 532484 | tf_op jit(solution)/shard_map/while/body/eval_jaxpr/reduce_sum | solution.py:54
  164.9 0.6 bitcast_dynamic-update-slice_fusion.2
  168.3 1.7 fusion.56
  170.0 18.6 %add.413 = f32[4,4,16,4,32,4]{5,4,3,2,1,0:T(8,128)} reshape(f32[1,16,64,128]{3,2,1,0:T(8,128)S(1)} %fusion.56) | data formatting | bytes 1048576 | tf_op jit(solution)/shard_map/while/body/eval_jaxpr/add | solution.py:62
  188.7 7.1 %reduce_sum.24 = f32[4,16,32]{2,1,0:T(8,128)S(1)} reduce(f32[4,4,16,4,32,4]{5,4,3,2,1,0:T(8,128)} %add.413, f32[]{:T(128)} %constant.123.clone.1..sunk), dimensions={1,3,5}, to_apply=%region_5.5 | reduce | flops 129024 | bytes 532484 | tf_op jit(solution)/shard_map/while/body/eval_jaxpr/reduce_sum | solution.py:54
  195.7 0.6 bitcast_dynamic-update-slice_fusion.2
  199.2 1.7 fusion.56
  200.8 18.6 %add.413 = f32[4,4,16,4,32,4]{5,4,3,2,1,0:T(8,128)} reshape(f32[1,16,64,128]{3,2,1,0:T(8,128)S(1)} %fusion.56) | data formatting | bytes 1048576 | tf_op jit(solution)/shard_map/while/body/eval_jaxpr/add | solution.py:62
  219.5 7.1 %reduce_sum.24 = f32[4,16,32]{2,1,0:T(8,128)S(1)} reduce(f32[4,4,16,4,32,4]{5,4,3,2,1,0:T(8,128)} %add.413, f32[]{:T(128)} %constant.123.clone.1..sunk), dimensions={1,3,5}, to_apply=%region_5.5 | reduce | flops 129024 | bytes 532484 | tf_op jit(solution)/shard_map/while/body/eval_jaxpr/reduce_sum | solution.py:54
  226.6 0.6 bitcast_dynamic-update-slice_fusion.2
  230.0 1.7 fusion.56
  231.7 18.6 %add.413 = f32[4,4,16,4,32,4]{5,4,3,2,1,0:T(8,128)} reshape(f32[1,16,64,128]{3,2,1,0:T(8,128)S(1)} %fusion.56) | data formatting | bytes 1048576 | tf_op jit(solution)/shard_map/while/body/eval_jaxpr/add | solution.py:62
  250.3 7.1 %reduce_sum.24 = f32[4,16,32]{2,1,0:T(8,128)S(1)} reduce(f32[4,4,16,4,32,4]{5,4,3,2,1,0:T(8,128)} %add.413, f32[]{:T(128)} %constant.123.clone.1..sunk), dimensions={1,3,5}, to_apply=%region_5.5 | reduce | flops 129024 | bytes 532484 | tf_op jit(solution)/shard_map/while/body/eval_jaxpr/reduce_sum | solution.py:54
  257.4 0.6 bitcast_dynamic-update-slice_fusion.2
  260.8 1.7 fusion.56
  262.5 18.6 %add.413 = f32[4,4,16,4,32,4]{5,4,3,2,1,0:T(8,128)} reshape(f32[1,16,64,128]{3,2,1,0:T(8,128)S(1)} %fusion.56) | data formatting | bytes 1048576 | tf_op jit(solution)/shard_map/while/body/eval_jaxpr/add | solution.py:62
  281.1 7.1 %reduce_sum.24 = f32[4,16,32]{2,1,0:T(8,128)S(1)} reduce(f32[4,4,16,4,32,4]{5,4,3,2,1,0:T(8,128)} %add.413, f32[]{:T(128)} %constant.123.clone.1..sunk), dimensions={1,3,5}, to_apply=%region_5.5 | reduce | flops 129024 | bytes 532484 | tf_op jit(solution)/shard_map/while/body/eval_jaxpr/reduce_sum | solution.py:54
  291.6 1.7 fusion.56
  293.3 18.6 %add.413 = f32[4,4,16,4,32,4]{5,4,3,2,1,0:T(8,128)} reshape(f32[1,16,64,128]{3,2,1,0:T(8,128)S(1)} %fusion.56) | data formatting | bytes 1048576 | tf_op jit(solution)/shard_map/while/body/eval_jaxpr/add | solution.py:62
  311.9 7.1 %reduce_sum.24 = f32[4,16,32]{2,1,0:T(8,128)S(1)} reduce(f32[4,4,16,4,32,4]{5,4,3,2,1,0:T(8,128)} %add.413, f32[]{:T(128)} %constant.123.clone.1..sunk), dimensions={1,3,5}, to_apply=%region_5.5 | reduce | flops 129024 | bytes 532484 | tf_op jit(solution)/shard_map/while/body/eval_jaxpr/reduce_sum | solution.py:54
  319.0 0.6 bitcast_dynamic-update-slice_fusion.2
  322.4 1.7 fusion.56
  324.1 18.6 %add.413 = f32[4,4,16,4,32,4]{5,4,3,2,1,0:T(8,128)} reshape(f32[1,16,64,128]{3,2,1,0:T(8,128)S(1)} %fusion.56) | data formatting | bytes 1048576 | tf_op jit(solution)/shard_map/while/body/eval_jaxpr/add | solution.py:62
  342.8 7.1 %reduce_sum.24 = f32[4,16,32]{2,1,0:T(8,128)S(1)} reduce(f32[4,4,16,4,32,4]{5,4,3,2,1,0:T(8,128)} %add.413, f32[]{:T(128)} %constant.123.clone.1..sunk), dimensions={1,3,5}, to_apply=%region_5.5 | reduce | flops 129024 | bytes 532484 | tf_op jit(solution)/shard_map/while/body/eval_jaxpr/reduce_sum | solution.py:54
  349.8 0.6 bitcast_dynamic-update-slice_fusion.2
  350.5 68.1 %all-gather.3.cloned.1.call-done = f32[144,4,16,32]{3,2,1,0:T(8,128)} async-done(((f32[9,4,16,32]{3,2,1,0:T(8,128)}), f32[144,4,16,32]{3,2,1,0:T(8,128)}) %all-gather.3.cloned.1.call-update) | async-done | bytes 1179664 | tf_op jit(solution)/shard_map/all_gather | solution.py:12
  418.6 2.9 reduce_sum.22
  421.5 14.2 %collective-permute-start.6 = (f32[9,1,16,32]{3,2,1,0:T(8,128)S(1)}, f32[9,1,16,32]{3,2,1,0:T(8,128)S(1)}, u32[]{:S(2)}, u32[]{:S(2)}) collective-permute-start(f32[9,1,16,32]{3,2,1,0:T(8,128)S(1)} %get-tuple-element.88), channel_id=1, source_target_pairs={{0,1},{1,2},{2,3},{3,4},{4,5},{5,6},{6,7},{7,8},{8,9},{9,10},{10,1... | collective-permute-start | bytes 55304 | tf_op jit(solution)/shard_map/ppermute | solution.py:24
  435.7 1.9 collective-permute-start.7
  437.8 7.2 %collective-permute-done.7 = f32[9,1,16,32]{3,2,1,0:T(8,128)S(1)} collective-permute-done((f32[9,1,16,32]{3,2,1,0:T(8,128)S(1)}, f32[9,1,16,32]{3,2,1,0:T(8,128)S(1)}, u32[]{:S(2)}, u32[]{:S(2)}) %collective-permute-start.7) | collective-permute-done | bytes 18464 | tf_op jit(solution)/shard_map/ppermute | solution.py:27
  447.2 0.7 copy.94
  (68 shorter events, 8.8 us)
Async XLA Ops:
  6.5 19.2 %copy-start = (f32[16,64,128]{2,1,0:T(8,128)S(1)}, f32[16,64,128]{2,1,0:T(8,128)}, u32[]{:S(2)}) copy-start(f32[16,64,128]{2,1,0:T(8,128)} %param.18) | copy-start | bytes 1572868
  6.5 412.0 %all-gather.3.cloned.1.call-start = ((), (), s32[]{:S(2)}) async-start(), calls=%async_computation | async-start | bytes 5013504 | tf_op jit(solution)/shard_map/all_gather | solution.py:12
  8.8 17.0 %collective-permute-start = (f32[2,1,64,128]{3,2,1,0:T(8,128)S(1)}, f32[2,1,64,128]{3,2,1,0:T(8,128)S(1)}, u32[]{:S(2)}, u32[]{:S(2)}) collective-permute-start(f32[2,1,64,128]{3,2,1,0:T(8,128)S(1)} %get-tuple-element.85), channel_id=1, source_target_pairs={{1,0},{2,1},{3,2},{4,3},{5,4},{6,5},{7,6},{8,7},{9,8},{10,9},{11,1... | collective-permute-start | bytes 196616 | tf_op jit(solution)/shard_map/ppermute | solution.py:27
  11.4 14.4 %collective-permute-start.1 = (f32[2,1,64,128]{3,2,1,0:T(8,128)S(1)}, f32[2,1,64,128]{3,2,1,0:T(8,128)S(1)}, u32[]{:S(2)}, u32[]{:S(2)}) collective-permute-start(f32[2,1,64,128]{3,2,1,0:T(8,128)S(1)} %get-tuple-element.86), channel_id=1, source_target_pairs={{0,1},{1,2},{2,3},{3,4},{4,5},{5,6},{6,7},{7,8},{8,9},{9,10},{10,1... | collective-permute-start | bytes 196616 | tf_op jit(solution)/shard_map/ppermute | solution.py:24
  27.7 14.8 %collective-permute-start.2 = (f32[2,1,64,128]{3,2,1,0:T(8,128)S(1)}, f32[2,1,64,128]{3,2,1,0:T(8,128)S(1)}, u32[]{:S(2)}, u32[]{:S(2)}) collective-permute-start(f32[2,1,64,128]{3,2,1,0:T(8,128)S(1)} %get-tuple-element.83), channel_id=1, source_target_pairs={{1,0},{2,1},{3,2},{4,3},{5,4},{6,5},{7,6},{8,7},{9,8},{10,9},{11,1... | collective-permute-start | bytes 196616 | tf_op jit(solution)/shard_map/ppermute | solution.py:27
  29.7 12.9 %collective-permute-start.3 = (f32[2,1,64,128]{3,2,1,0:T(8,128)S(1)}, f32[2,1,64,128]{3,2,1,0:T(8,128)S(1)}, u32[]{:S(2)}, u32[]{:S(2)}) collective-permute-start(f32[2,1,64,128]{3,2,1,0:T(8,128)S(1)} %get-tuple-element.84), channel_id=1, source_target_pairs={{0,1},{1,2},{2,3},{3,4},{4,5},{5,6},{6,7},{7,8},{8,9},{9,10},{10,1... | collective-permute-start | bytes 196616 | tf_op jit(solution)/shard_map/ppermute | solution.py:24
  45.7 15.6 %collective-permute-start.4 = (f32[4,8,64,128]{3,2,1,0:T(8,128)}, f32[4,8,64,128]{3,2,1,0:T(8,128)}, u32[]{:S(2)}, u32[]{:S(2)}) collective-permute-start(f32[4,8,64,128]{3,2,1,0:T(8,128)} %get-tuple-element.81), channel_id=1, source_target_pairs={{0,1},{1,2},{2,3},{3,4},{4,5},{5,6},{6,7},{7,8},{8,9},{9,10},{10,1... | collective-permute-start | bytes 3145736 | tf_op jit(solution)/shard_map/ppermute | solution.py:24
  49.2 19.8 %collective-permute-start.5 = (f32[4,8,64,128]{3,2,1,0:T(8,128)S(1)}, f32[4,8,64,128]{3,2,1,0:T(8,128)}, u32[]{:S(2)}, u32[]{:S(2)}) collective-permute-start(f32[4,8,64,128]{3,2,1,0:T(8,128)S(1)} %get-tuple-element.82), channel_id=1, source_target_pairs={{1,0},{2,1},{3,2},{4,3},{5,4},{6,5},{7,6},{8,7},{9,8},{10,9},{11,1... | collective-permute-start | bytes 3145736 | tf_op jit(solution)/shard_map/ppermute | solution.py:27
  51.2 21.9 %copy-start.3 = (s32[9]{0:T(128)S(1)}, s32[9]{0:T(128)}, u32[]{:S(2)}) copy-start(s32[9]{0:T(128)} %param.23) | copy-start | bytes 112
  350.4 87.3 %copy-start.1 = (f32[64,9,3,3,3]{0,4,3,2,1:T(4,128)S(1)}, f32[64,9,3,3,3]{0,4,3,2,1:T(4,128)}, u32[]{:S(2)}) copy-start(f32[64,9,3,3,3]{0,4,3,2,1:T(4,128)} %param.24) | copy-start | bytes 186628
  418.6 28.3 %copy-start.2 = (f32[64]{0:T(128)S(1)}, f32[64]{0:T(128)}, u32[]{:S(2)}) copy-start(f32[64]{0:T(128)} %param.25) | copy-start | bytes 772
  421.5 16.3 %collective-permute-start.6 = (f32[9,1,16,32]{3,2,1,0:T(8,128)S(1)}, f32[9,1,16,32]{3,2,1,0:T(8,128)S(1)}, u32[]{:S(2)}, u32[]{:S(2)}) collective-permute-start(f32[9,1,16,32]{3,2,1,0:T(8,128)S(1)} %get-tuple-element.88), channel_id=1, source_target_pairs={{0,1},{1,2},{2,3},{3,4},{4,5},{5,6},{6,7},{7,8},{8,9},{9,10},{10,1... | collective-permute-start | bytes 55304 | tf_op jit(solution)/shard_map/ppermute | solution.py:24
  435.7 9.3 %collective-permute-start.7 = (f32[9,1,16,32]{3,2,1,0:T(8,128)S(1)}, f32[9,1,16,32]{3,2,1,0:T(8,128)S(1)}, u32[]{:S(2)}, u32[]{:S(2)}) collective-permute-start(f32[9,1,16,32]{3,2,1,0:T(8,128)S(1)} %get-tuple-element.87), channel_id=1, source_target_pairs={{1,0},{2,1},{3,2},{4,3},{5,4},{6,5},{7,6},{8,7},{9,8},{10,9},{11,1... | collective-permute-start | bytes 55304 | tf_op jit(solution)/shard_map/ppermute | solution.py:27
Sparse Core Ops, SparseCore 0:
  350.6 67.9 all-gather.2
